TPU v7x, 512 devices: a whole 4x8x8 slice. The times are simulated.
512 devices in a mesh: src: 32 (over y, x_lo, core), rcv: 8 (over z), int: 2 (over x_hi).
Axes of the slice: x: 4 (x_hi: 2, x_lo: 2; x = x_hi * 2 + x_lo), y: 8, z: 8, core: 2. Of those that a mesh axis runs over, the one named last changes fastest.
Arguments:
- traces: float32 [2, 1, 4096, 4096], P(None, None, 'src', 'rcv'), may hold values from -6 to 6
- missing: int32 [32, 32], P('src', 'rcv'), may hold values from 0 to 1, as said below
- aperture: int32 [32, 24], P('src'), may hold values from 0 to 32, as said below
- wavelet: float32 [2, 1], replicated, may hold values from -0.06 to 0.06
Outputs:
- primaries: float32 [2, 1, 4096, 4096], P(None, None, 'src', ('rcv', 'int'))
Inputs may be any that keep to these rules, and one draw needn't show every extreme that they name: `missing`: A tile is marked only where its receiver block lies above its source block, so the mirrored tile is always recorded; some tile is marked. `aperture`: in each row the listed blocks come first and are distinct; the remaining entries are the padding value 32. Each row lists 24 // 2 to 24 blocks; some row lists exactly 24 and some row exactly 12.
All inputs are finite; a program needn't handle non-finite values.
Results may differ from a plain program's by a relative error of at most 0.00005.
Values sent between devices are 32-bit elements; how exact they have to be, the bound alone decides.
No kernel may reach another device: no remote copies, remote signals or barrier semaphores. Data moves between devices by JAX's collectives and lax.ppermute only.
A program may use at most 64 MiB of HBM per device.

v0:
```python
import jax
import jax.numpy as jnp
import numpy as np
from jax import lax
from jax.sharding import Mesh
from jax.sharding import PartitionSpec as P

TILE = 128
SRC = ("y", "xl", "c")
FILL = ("y", "xl", "c", "z")


def mirror_pairs(n_src, n_rcv, per_rcv, step):
    pairs = []
    for s in range(n_src):
        for r in range(n_rcv):
            t = (s % per_rcv + step) % per_rcv
            dest_s = per_rcv * r + t
            if s > dest_s:
                pairs.append((s * n_rcv + r, dest_s * n_rcv + s // per_rcv))
    return pairs


def per_device(traces, missing, aperture, wavelet):
    n_src = lax.axis_size(SRC)
    n_rcv = lax.axis_size("z")
    n_half = lax.axis_size("xh")
    n_core = lax.axis_size("c")
    me_src = lax.axis_index(SRC)
    me_rcv = lax.axis_index("z")
    my_half = lax.axis_index("xh")
    comp_count, freq_count, local_rows, local_cols = traces.shape
    assert local_rows == TILE
    per_rcv = local_cols // TILE
    tiles = traces.reshape(comp_count, freq_count, TILE, per_rcv, TILE)
    arrived = []
    for step in range(per_rcv):
        pick = (me_src % per_rcv + step) % per_rcv
        sent = lax.dynamic_index_in_dim(tiles, pick, 3, keepdims=False)
        got = lax.ppermute(sent, FILL, mirror_pairs(n_src, n_rcv, per_rcv, step))
        arrived.append(jnp.swapaxes(got, 2, 3))
    arrived = jnp.stack(arrived, axis=3)
    order = (me_src % per_rcv - jnp.arange(per_rcv)) % per_rcv
    mirrored = jnp.take(arrived, order, axis=3)
    marks = (missing[0] > 0)[None, None, None, :, None]
    filled = jnp.where(marks, mirrored, tiles)
    first = me_rcv * per_rcv
    local_blocks = first + jnp.arange(per_rcv, dtype=jnp.int32)
    chosen = (aperture[0][:, None] == local_blocks[None, :]).astype(jnp.float32).sum(axis=0)
    half = TILE // n_half
    left = filled.reshape(comp_count, freq_count, TILE, per_rcv, n_half, half)
    left = lax.dynamic_index_in_dim(left, my_half, 4, keepdims=False)
    left = left * chosen[None, None, None, :, None]
    left = left.reshape(comp_count, freq_count, TILE, per_rcv * half)
    left = lax.all_gather(left, "z", axis=3, tiled=True)
    n_pair = n_src // n_core
    left = left.reshape(comp_count, freq_count, TILE, n_pair, n_core, half)
    left = jnp.transpose(left, (1, 0, 2, 4, 3, 5))
    left = left.reshape(freq_count, comp_count * TILE, n_src * half)
    right = filled.reshape(comp_count, freq_count, n_half, half, local_cols)
    right = lax.dynamic_index_in_dim(right, my_half, 2, keepdims=False)
    right = jnp.transpose(right, (1, 2, 0, 3))
    right = lax.all_gather(right, ("y", "xl"), axis=1, tiled=True)
    right = lax.all_gather(right, "c", axis=1, tiled=False)
    right = right.reshape(freq_count, n_src * half, comp_count * local_cols)
    prod = jnp.einsum("fak,fkb->fab", left, right, precision=lax.Precision.HIGHEST)
    prod = prod.reshape(freq_count, comp_count, TILE, comp_count, local_cols)
    real_part = prod[:, 0, :, 0] - prod[:, 1, :, 1]
    imag_part = prod[:, 0, :, 1] + prod[:, 1, :, 0]
    partial_sum = jnp.stack([real_part, imag_part])
    my_share = lax.psum_scatter(partial_sum, "xh", scatter_dimension=3, tiled=True)
    out_cols = local_cols // n_half
    kept = filled.reshape(comp_count, freq_count, TILE, local_cols)
    kept = lax.dynamic_slice_in_dim(kept, my_half * out_cols, out_cols, axis=3)
    w_real = wavelet[0][:, None, None]
    w_imag = wavelet[1][:, None, None]
    out_real = kept[0] - (w_real * my_share[0] - w_imag * my_share[1])
    out_imag = kept[1] - (w_real * my_share[1] + w_imag * my_share[0])
    return jnp.stack([out_real, out_imag])


def solution(mesh):
    n_src, n_rcv, n_int = (mesh.shape[a] for a in ("src", "rcv", "int"))
    fine = Mesh(
        np.asarray(mesh.devices).reshape(n_src // 4, 2, 2, n_rcv, n_int),
        ("y", "xl", "c", "z", "xh"),
    )
    placed = (P(None, None, SRC, "z"), P(SRC, "z"), P(SRC, None), P())
    return jax.shard_map(
        per_device,
        mesh=fine,
        in_specs=placed,
        out_specs=P(None, None, SRC, ("z", "xh")),
        check_vma=False,
    )
```

profile of v0, /device:TPU:1, one launch (start us, length us, event | category | flops | bytes accessed | tf_op | source)
XLA Modules:
  0.0 325.5 jit_solution(12362574936343730955)
XLA Ops:
  6.5 0.0 copy-start
  6.5 0.0 copy-start.2
  6.5 0.0 all-gather.7.cloned.1.call-start
  6.5 1.3 reshape.249
  7.8 0.5 constant_dynamic-slice_fusion.3
  8.3 0.1 copy.56
  8.4 8.8 %collective-permute-start.3 = (f32[2,1,128,128]{2,3,0,1:T(8,128)S(1)}, f32[2,1,128,128]{2,3,0,1:T(8,128)S(1)}, u32[]{:S(2)}, u32[]{:S(2)}) collective-permute-start(f32[2,1,128,128]{2,3,0,1:T(8,128)S(1)} %bitcast.75), channel_id=1, source_target_pairs={{16,0},{32,16},{48,32},{64,50},{80,2},{82,66},{96,18},{98,82},{112... | collective-permute-start | bytes 393224 | tf_op jit(solution)/shard_map/ppermute | solution.py:40
  17.2 0.1 copy.54
  17.3 0.7 collective-permute-start.1
  18.0 0.1 copy.55
  18.1 1.3 collective-permute-start.2
  19.4 0.1 copy.53
  19.5 0.7 collective-permute-start
  20.2 0.7 compare_bitcast_fusion
  20.8 0.1 broadcast_bitcast_fusion
  21.0 0.0 collective-permute-done.3
  21.0 0.0 collective-permute-done.1
  21.0 4.1 %collective-permute-done.2 = f32[2,1,128,128]{2,3,0,1:T(8,128)S(1)} collective-permute-done((f32[2,1,128,128]{2,3,0,1:T(8,128)S(1)}, f32[2,1,128,128]{2,3,0,1:T(8,128)S(1)}, u32[]{:S(2)}, u32[]{:S(2)}) %collective-permute-start.2) | collective-permute-done | bytes 131104 | tf_op jit(solution)/shard_map/ppermute | solution.py:40
  25.1 0.0 collective-permute-done
  25.1 0.6 gather_fusion
  25.7 0.3 copy.42
  26.1 0.2 gather.13
  26.3 1.7 fusion.2
  28.0 0.0 all-gather.7.cloned.1.call-update
  28.0 0.0 all-gather.5.cloned.1.call-start
  28.1 0.0 copy-done
  28.1 0.2 copy.44
  28.3 0.0 copy-done.2
  28.3 0.2 convert_reduce_fusion
  28.5 0.1 mul.83
  28.6 0.1 mul.84
  28.7 0.2 copy.43
  28.9 0.1 dynamic-slice_select_fusion.2
  29.0 0.8 bitcast_multiply_fusion
  29.8 0.0 all-gather.5.cloned.1.call-update
  29.8 0.0 all-gather.9.cloned.1.call-start
  29.8 138.6 %all-gather.7.cloned.1.call-done = f32[1,1024,2,512]{3,1,2,0:T(8,128)} async-done(((f32[1,64,2,512]{3,1,2,0:T(8,128)}), f32[1,1024,2,512]{3,1,2,0:T(8,128)}) %all-gather.7.cloned.1.call-update) | async-done | bytes 4194320 | tf_op jit(solution)/shard_map/all_gather | solution.py:63
  168.4 0.0 all-gather.9.cloned.1.call-update
  168.5 0.2 reduce-scatter.2.cloned.1.call-start
  168.7 43.9 %all-gather.5.cloned.1.call-done = f32[2,1,128,2048]{2,3,0,1:T(8,128)} async-done(((f32[2,1,128,256]{2,3,0,1:T(8,128)}), f32[2,1,128,2048]{2,3,0,1:T(8,128)}) %all-gather.5.cloned.1.call-update) | async-done | bytes 2097168 | tf_op jit(solution)/shard_map/all_gather | solution.py:55
  212.6 1.7 copy.45
  214.3 32.0 %all-gather.9.cloned.1.call-done = f32[2,1024,2,512]{3,1,2,0:T(8,128)} async-done(((f32[1,1024,2,512]{3,1,2,0:T(8,128)}), f32[2,1024,2,512]{3,1,2,0:T(8,128)}) %all-gather.9.cloned.1.call-update) | async-done | bytes 8388624 | tf_op jit(solution)/shard_map/all_gather | solution.py:64
  246.3 14.4 %copy.47 = f32[2,1024,2,512]{3,2,1,0:T(2,128)S(1)} copy(f32[2,1024,2,512]{3,1,2,0:T(8,128)} %all-gather.9.cloned.1.call-done) | data formatting | bytes 16777216 | tf_op jit(solution)/shard_map/all_gather | solution.py:64
  260.7 5.3 %copy.57 = f32[256,8,2,512]{3,1,2,0:T(8,128)} copy(f32[256,8,2,512]{3,2,1,0:T(2,128)S(1)} %bitcast.66) | data formatting | bytes 16777216
  266.0 9.2 %copy.48 = f32[1024,2048]{1,0:T(8,128)} copy(f32[1024,2048]{0,1:T(8,128)} %bitcast.67) | data formatting | bytes 16777216 | tf_op jit(solution)/shard_map/fak,fkb->fab/dot_general | solution.py:66
  275.3 0.0 copy-start.1
  275.3 15.8 %convolution_bitcast_fusion = f32[1,2,128,2,512]{4,2,3,1,0:T(8,128)S(1)} fusion(f32[2,128,2048,1]{1,2,3,0:T(8,128)S(1)} %bitcast.68, f32[2,512,2048,1]{2,1,0,3:T(8,128)} %bitcast.65), kind=kOutput, calls=%fused_computation.1 | convolution fusion | flops 6442450944 | bytes 11534336 | tf_op jit(solution)/shard_map/fak,fkb->fab/dot_general | solution.py:66
  291.1 0.1 fusion.1
  291.2 0.8 pad_maximum_fusion
  292.0 0.0 reduce-scatter.2.cloned.1.call-update
  292.0 0.1 dynamic-slice
  292.1 0.1 dynamic-slice.1
  292.2 0.0 copy-done.1
  292.2 0.6 fusion.6
  292.8 0.2 gather.11
  293.0 0.1 dynamic-slice_select_fusion.4
  293.1 22.8 %reduce-scatter.2.cloned.1.call-done = f32[2,1,128,256]{3,2,1,0:T(8,128)} async-done(((f32[2,1,128,512]{3,2,1,0:T(8,128)}), f32[2,1,128,256]{3,2,1,0:T(8,128)}) %reduce-scatter.2.cloned.1.call-update) | async-done | bytes 262160 | tf_op jit(solution)/shard_map/reduce_scatter | solution.py:71
  315.9 2.3 slice_subtract_fusion.2
  318.2 0.7 pad_maximum_fusion.1
  (5 shorter events, 0.1 us)
Async XLA Ops:
  6.5 21.5 %copy-start = (f32[2,1,128,512]{3,2,1,0:T(8,128)S(1)}, f32[2,1,128,512]{3,2,1,0:T(8,128)}, u32[]{:S(2)}) copy-start(f32[2,1,128,512]{3,2,1,0:T(8,128)} %param.4) | copy-start | bytes 1572868
  6.5 21.8 %copy-start.2 = (s32[1,24]{1,0:T(1,128)S(1)}, s32[1,24]{1,0:T(1,128)}, u32[]{:S(2)}) copy-start(s32[1,24]{1,0:T(1,128)} %param.6) | copy-start | bytes 292
  6.5 161.9 %all-gather.7.cloned.1.call-start = ((), (), s32[]{:S(2)}) async-start(), calls=%async_computation.2 | async-start | bytes 4456448 | tf_op jit(solution)/shard_map/all_gather | solution.py:63
  8.4 12.5 %collective-permute-start.3 = (f32[2,1,128,128]{2,3,0,1:T(8,128)S(1)}, f32[2,1,128,128]{2,3,0,1:T(8,128)S(1)}, u32[]{:S(2)}, u32[]{:S(2)}) collective-permute-start(f32[2,1,128,128]{2,3,0,1:T(8,128)S(1)} %bitcast.75), channel_id=1, source_target_pairs={{16,0},{32,16},{48,32},{64,50},{80,2},{82,66},{96,18},{98,82},{112... | collective-permute-start | bytes 393224 | tf_op jit(solution)/shard_map/ppermute | solution.py:40
  17.3 3.7 %collective-permute-start.1 = (f32[2,1,128,128]{2,3,0,1:T(8,128)S(1)}, f32[2,1,128,128]{2,3,0,1:T(8,128)S(1)}, u32[]{:S(2)}, u32[]{:S(2)}) collective-permute-start(f32[2,1,128,128]{2,3,0,1:T(8,128)S(1)} %bitcast.76), channel_id=1, source_target_pairs={{48,0},{64,18},{80,34},{96,50},{112,2},{114,66},{128,20},{130,84},... | collective-permute-start | bytes 393224 | tf_op jit(solution)/shard_map/ppermute | solution.py:40
  18.1 7.0 %collective-permute-start.2 = (f32[2,1,128,128]{2,3,0,1:T(8,128)S(1)}, f32[2,1,128,128]{2,3,0,1:T(8,128)S(1)}, u32[]{:S(2)}, u32[]{:S(2)}) collective-permute-start(f32[2,1,128,128]{2,3,0,1:T(8,128)S(1)} %bitcast.77), channel_id=1, source_target_pairs={{32,0},{48,16},{64,34},{80,50},{96,2},{98,66},{112,18},{114,82},{1... | collective-permute-start | bytes 393224 | tf_op jit(solution)/shard_map/ppermute | solution.py:40
  19.5 5.6 %collective-permute-start = (f32[2,1,128,128]{2,3,0,1:T(8,128)S(1)}, f32[2,1,128,128]{2,3,0,1:T(8,128)S(1)}, u32[]{:S(2)}, u32[]{:S(2)}) collective-permute-start(f32[2,1,128,128]{2,3,0,1:T(8,128)S(1)} %bitcast.78), channel_id=1, source_target_pairs={{64,2},{80,18},{96,34},{112,50},{128,4},{130,68},{144,20},{146,84}... | collective-permute-start | bytes 393224 | tf_op jit(solution)/shard_map/ppermute | solution.py:40
  28.0 184.5 %all-gather.5.cloned.1.call-start = ((), (), s32[]{:S(2)}) async-start(), calls=%async_computation.1 | async-start | bytes 2359296 | tf_op jit(solution)/shard_map/all_gather | solution.py:55
  29.8 216.5 %all-gather.9.cloned.1.call-start = ((), (), s32[]{:S(2)}) async-start(), calls=%async_computation.4 | async-start | bytes 12582912 | tf_op jit(solution)/shard_map/all_gather | solution.py:64
  168.5 147.5 %reduce-scatter.2.cloned.1.call-start = ((), (), s32[]{:S(2)}) async-start(), calls=%async_computation.3 | async-start | bytes 786432 | tf_op jit(solution)/shard_map/reduce_scatter | solution.py:71
  275.3 16.9 %copy-start.1 = (f32[2,1]{0,1:T(1,128)S(1)}, f32[2,1]{0,1:T(1,128)}, u32[]{:S(2)}) copy-start(f32[2,1]{0,1:T(1,128)} %param.7) | copy-start | bytes 28
Sparse Core Ops, SparseCore 0:
  28.2 140.2 all-gather.6
  170.5 42.0 all-gather.4
  214.7 31.5 all-gather.8
  292.1 23.7 reduce-scatter.1
where the time goes:
time: 326 us; the launch traced here: 325 us
  waiting for transfers between devices  241 us (74%)
  local copies, waits for them, and re-layouts  35.6 us (11%)
  matrix products  15.8 us (5%)
  between operations  13.4 us (4%)
  starting transfers between devices  11.7 us (4%)
  other arithmetic  7.52 us (2%)
    all_gather x1, waiting for transfers between devices, per_device(): right = lax.all_gather(right, ('y', 'xl'), axis=1, tiled=True)  139 us
    all_gather x1, waiting for transfers between devices, per_device(): left = lax.all_gather(left, 'z', axis=3, tiled=True)  43.9 us
    all_gather x1, waiting for transfers between devices, per_device(): right = lax.all_gather(right, 'c', axis=1, tiled=False)  32 us
    reduce_scatter x1, waiting for transfers between devices, per_device(): lax.psum_scatter(partial_sum, 'xh', scatter_dimension=3, tiled=True)  22.8 us
    dot_general x1, matrix products, per_device(): jnp.einsum('fak,fkb->fab', left, right, precision=lax.Precision.HIGHEST)  15.8 us
    all_gather x1, local copies, waits for them, and re-layouts, per_device(): right = lax.all_gather(right, 'c', axis=1, tiled=False)  14.4 us
    ppermute x4, starting transfers between devices, per_device(): got = lax.ppermute(sent, FILL, mirror_pairs(n_src, n_rcv, per_rcv, step))  11.4 us
    dot_general x1, local copies, waits for them, and re-layouts, per_device(): jnp.einsum('fak,fkb->fab', left, right, precision=lax.Precision.HIGHEST)  9.22 us
  transfers between devices with their start and end apart: 8, of which 5 were waited for; matrix products, arithmetic and copies ran while one was open for 2% of the time, Pallas kernels for 0%

commit v1 on v0

--- a/solution.py
+++ b/solution.py
@@ -52,7 +52,9 @@
     left = lax.dynamic_index_in_dim(left, my_half, 4, keepdims=False)
     left = left * chosen[None, None, None, :, None]
     left = left.reshape(comp_count, freq_count, TILE, per_rcv * half)
-    left = lax.all_gather(left, "z", axis=3, tiled=True)
+    left = jnp.concatenate(
+        lax.all_to_all(jnp.stack([left] * lax.axis_size("z")), "z", 0, 0), axis=3
+    )
     n_pair = n_src // n_core
     left = left.reshape(comp_count, freq_count, TILE, n_pair, n_core, half)
     left = jnp.transpose(left, (1, 0, 2, 4, 3, 5))

time: 326 us -> 303 us (0.929)
  waiting for transfers between devices: 241 us -> 166 us
  blocking collectives: 0 us -> 56 us
    all_to_all x0 -> x1, blocking collectives: none -> 56 us  [per_device(): lax.all_to_all(jnp.stack([left] * lax.axis_size('z')), 'z', 0, 0)]
    all_gather x1 -> x0, waiting for transfers between devices: 43.9 us -> none  [per_device(): left = lax.all_gather(left, 'z', axis=3, tiled=True)]
    all_gather x1, waiting for transfers between devices: 32 us -> 0.02 us  [per_device(): right = lax.all_gather(right, 'c', axis=1, tiled=False)]
  transfers between devices with their start and end apart: 8 -> 7, of which waited for: 5 -> 3; matrix products, arithmetic and copies ran while one was open for 2% -> 1% of each run, Pallas kernels for 0% -> 0%
where the time goes in v1:
time: 303 us
  waiting for transfers between devices  166 us (55%)
  blocking collectives  56 us (18%)
  local copies, waits for them, and re-layouts  34.4 us (11%)
  matrix products  15.8 us (5%)
  between operations  13.4 us (4%)
  starting transfers between devices  11.5 us (4%)
  other arithmetic  5.9 us (2%)
    all_gather x1, waiting for transfers between devices, per_device(): right = lax.all_gather(right, ('y', 'xl'), axis=1, tiled=True)  140 us
    all_to_all x1, blocking collectives, per_device(): lax.all_to_all(jnp.stack([left] * lax.axis_size('z')), 'z', 0, 0)  56 us
    reduce_scatter x1, waiting for transfers between devices, per_device(): lax.psum_scatter(partial_sum, 'xh', scatter_dimension=3, tiled=True)  21.4 us
    dot_general x1, matrix products, per_device(): jnp.einsum('fak,fkb->fab', left, right, precision=lax.Precision.HIGHEST)  15.8 us
    all_gather x1, local copies, waits for them, and re-layouts, per_device(): right = lax.all_gather(right, 'c', axis=1, tiled=False)  14.4 us
    ppermute x4, starting transfers between devices, per_device(): got = lax.ppermute(sent, FILL, mirror_pairs(n_src, n_rcv, per_rcv, step))  11.4 us
    dot_general x1, local copies, waits for them, and re-layouts, per_device(): jnp.einsum('fak,fkb->fab', left, right, precision=lax.Precision.HIGHEST)  9.13 us
  transfers between devices with their start and end apart: 7, of which 3 were waited for; matrix products, arithmetic and copies ran while one was open for 1% of the time, Pallas kernels for 0%

profile of v1, /device:TPU:1, one launch (start us, length us, event | category | flops | bytes accessed | tf_op | source)
XLA Modules:
  0.0 303.0 jit_solution(50450297979556376)
XLA Ops:
  6.5 0.0 copy-start
  6.5 0.0 all-gather.4.cloned.1.call-start
  6.5 1.3 reshape.246
  7.8 0.5 constant_dynamic-slice_fusion.3
  8.3 0.1 copy.58
  8.4 8.8 %collective-permute-start.3 = (f32[2,1,128,128]{2,3,0,1:T(8,128)S(1)}, f32[2,1,128,128]{2,3,0,1:T(8,128)S(1)}, u32[]{:S(2)}, u32[]{:S(2)}) collective-permute-start(f32[2,1,128,128]{2,3,0,1:T(8,128)S(1)} %bitcast.77), channel_id=1, source_target_pairs={{16,0},{32,16},{48,32},{64,50},{80,2},{82,66},{96,18},{98,82},{112... | collective-permute-start | bytes 393224 | tf_op jit(solution)/shard_map/ppermute | solution.py:40
  17.2 0.1 copy.56
  17.3 0.7 collective-permute-start.1
  18.0 0.1 copy.57
  18.1 1.3 collective-permute-start.2
  19.4 0.1 copy.55
  19.5 0.7 collective-permute-start
  20.2 0.7 compare_bitcast_fusion
  20.8 0.1 broadcast_bitcast_fusion
  21.0 0.0 collective-permute-done.3
  21.0 0.0 collective-permute-done.1
  21.0 4.1 %collective-permute-done.2 = f32[2,1,128,128]{2,3,0,1:T(8,128)S(1)} collective-permute-done((f32[2,1,128,128]{2,3,0,1:T(8,128)S(1)}, f32[2,1,128,128]{2,3,0,1:T(8,128)S(1)}, u32[]{:S(2)}, u32[]{:S(2)}) %collective-permute-start.2) | collective-permute-done | bytes 131104 | tf_op jit(solution)/shard_map/ppermute | solution.py:40
  25.1 0.0 collective-permute-done
  25.1 0.6 gather_fusion
  25.7 0.0 copy-start.2
  25.7 0.3 copy.43
  26.1 0.2 gather.13
  26.3 0.0 copy-done
  26.3 0.7 fusion.2
  27.1 0.0 all-gather.4.cloned.1.call-update
  27.1 0.0 all-gather.6.cloned.1.call-start
  27.1 140.3 %all-gather.4.cloned.1.call-done = f32[1,1024,2,512]{3,1,2,0:T(8,128)} async-done(((f32[1,64,2,512]{3,1,2,0:T(8,128)}), f32[1,1024,2,512]{3,1,2,0:T(8,128)}) %all-gather.4.cloned.1.call-update) | async-done | bytes 4194320 | tf_op jit(solution)/shard_map/all_gather | solution.py:65
  167.5 0.0 all-gather.6.cloned.1.call-update
  167.5 0.0 reduce-scatter.2.cloned.1.call-start
  167.6 0.2 copy.45
  167.8 0.0 copy-done.2
  167.8 0.2 convert_reduce_fusion
  168.0 0.1 mul.81
  168.0 0.1 mul.82
  168.1 0.2 copy.44
  168.3 0.1 dynamic-slice_select_fusion.2
  168.4 0.1 broadcast_multiply_fusion
  168.5 0.2 stack.33
  168.8 56.0 %all_to_all.5 = f32[8,2,1,128,256]{3,4,1,2,0:T(8,128)S(1)} all-to-all(f32[8,2,1,128,256]{3,4,1,2,0:T(8,128)S(1)} %stack.33), channel_id=1, replica_groups=mesh['y'=8,'xl'=2,'c'=2,'z'=8,'xh'=2] {'z'}, dimensions={0} | all-to-all | bytes 4194304 | tf_op jit(solution)/shard_map/all_to_all | solution.py:56
  224.8 0.2 copy.46
  225.0 0.2 copy.47
  225.2 0.0 all-gather.6.cloned.1.call-done
  225.3 14.4 %copy.49 = f32[2,1024,2,512]{3,2,1,0:T(2,128)S(1)} copy(f32[2,1024,2,512]{3,1,2,0:T(8,128)} %all-gather.6.cloned.1.call-done) | data formatting | bytes 16777216 | tf_op jit(solution)/shard_map/all_gather | solution.py:66
  239.7 5.3 %copy.59 = f32[256,8,2,512]{3,1,2,0:T(8,128)} copy(f32[256,8,2,512]{3,2,1,0:T(2,128)S(1)} %bitcast.67) | data formatting | bytes 16777216
  245.0 9.1 %copy.50 = f32[1024,2048]{1,0:T(8,128)} copy(f32[1024,2048]{0,1:T(8,128)} %bitcast.68) | data formatting | bytes 16777216 | tf_op jit(solution)/shard_map/fak,fkb->fab/dot_general | solution.py:68
  254.1 0.0 copy-start.1
  254.1 15.8 %convolution_bitcast_fusion = f32[1,2,128,2,512]{4,2,3,1,0:T(8,128)S(1)} fusion(f32[2,128,2048,1]{1,2,3,0:T(8,128)S(1)} %bitcast.70, f32[2,512,2048,1]{2,1,0,3:T(8,128)} %bitcast.66), kind=kOutput, calls=%fused_computation.1 | convolution fusion | flops 6442450944 | bytes 11534336 | tf_op jit(solution)/shard_map/fak,fkb->fab/dot_general | solution.py:68
  269.9 0.1 fusion.1
  270.0 0.8 pad_maximum_fusion
  270.9 0.0 reduce-scatter.2.cloned.1.call-update
  270.9 0.1 dynamic-slice
  271.0 0.1 dynamic-slice.1
  271.0 0.0 copy-done.1
  271.0 0.7 fusion.6
  271.7 0.2 gather.11
  271.9 0.1 dynamic-slice_select_fusion.4
  272.0 21.4 %reduce-scatter.2.cloned.1.call-done = f32[2,1,128,256]{3,2,1,0:T(8,128)} async-done(((f32[2,1,128,512]{3,2,1,0:T(8,128)}), f32[2,1,128,256]{3,2,1,0:T(8,128)}) %reduce-scatter.2.cloned.1.call-update) | async-done | bytes 262160 | tf_op jit(solution)/shard_map/reduce_scatter | solution.py:73
  293.4 2.3 slice_subtract_fusion.2
  295.8 0.7 pad_maximum_fusion.1
  (5 shorter events, 0.1 us)
Async XLA Ops:
  6.5 19.8 %copy-start = (f32[2,1,128,512]{3,2,1,0:T(8,128)S(1)}, f32[2,1,128,512]{3,2,1,0:T(8,128)}, u32[]{:S(2)}) copy-start(f32[2,1,128,512]{3,2,1,0:T(8,128)} %param.4) | copy-start | bytes 1572868
  6.5 161.0 %all-gather.4.cloned.1.call-start = ((), (), s32[]{:S(2)}) async-start(), calls=%async_computation.2 | async-start | bytes 4456448 | tf_op jit(solution)/shard_map/all_gather | solution.py:65
  8.4 12.5 %collective-permute-start.3 = (f32[2,1,128,128]{2,3,0,1:T(8,128)S(1)}, f32[2,1,128,128]{2,3,0,1:T(8,128)S(1)}, u32[]{:S(2)}, u32[]{:S(2)}) collective-permute-start(f32[2,1,128,128]{2,3,0,1:T(8,128)S(1)} %bitcast.77), channel_id=1, source_target_pairs={{16,0},{32,16},{48,32},{64,50},{80,2},{82,66},{96,18},{98,82},{112... | collective-permute-start | bytes 393224 | tf_op jit(solution)/shard_map/ppermute | solution.py:40
  17.3 3.7 %collective-permute-start.1 = (f32[2,1,128,128]{2,3,0,1:T(8,128)S(1)}, f32[2,1,128,128]{2,3,0,1:T(8,128)S(1)}, u32[]{:S(2)}, u32[]{:S(2)}) collective-permute-start(f32[2,1,128,128]{2,3,0,1:T(8,128)S(1)} %bitcast.78), channel_id=1, source_target_pairs={{48,0},{64,18},{80,34},{96,50},{112,2},{114,66},{128,20},{130,84},... | collective-permute-start | bytes 393224 | tf_op jit(solution)/shard_map/ppermute | solution.py:40
  18.1 7.0 %collective-permute-start.2 = (f32[2,1,128,128]{2,3,0,1:T(8,128)S(1)}, f32[2,1,128,128]{2,3,0,1:T(8,128)S(1)}, u32[]{:S(2)}, u32[]{:S(2)}) collective-permute-start(f32[2,1,128,128]{2,3,0,1:T(8,128)S(1)} %bitcast.79), channel_id=1, source_target_pairs={{32,0},{48,16},{64,34},{80,50},{96,2},{98,66},{112,18},{114,82},{1... | collective-permute-start | bytes 393224 | tf_op jit(solution)/shard_map/ppermute | solution.py:40
  19.5 5.6 %collective-permute-start = (f32[2,1,128,128]{2,3,0,1:T(8,128)S(1)}, f32[2,1,128,128]{2,3,0,1:T(8,128)S(1)}, u32[]{:S(2)}, u32[]{:S(2)}) collective-permute-start(f32[2,1,128,128]{2,3,0,1:T(8,128)S(1)} %bitcast.80), channel_id=1, source_target_pairs={{64,2},{80,18},{96,34},{112,50},{128,4},{130,68},{144,20},{146,84}... | collective-permute-start | bytes 393224 | tf_op jit(solution)/shard_map/ppermute | solution.py:40
  25.7 142.0 %copy-start.2 = (s32[1,24]{1,0:T(1,128)S(1)}, s32[1,24]{1,0:T(1,128)}, u32[]{:S(2)}) copy-start(s32[1,24]{1,0:T(1,128)} %param.6) | copy-start | bytes 292
  27.1 198.2 %all-gather.6.cloned.1.call-start = ((), (), s32[]{:S(2)}) async-start(), calls=%async_computation.4 | async-start | bytes 12582912 | tf_op jit(solution)/shard_map/all_gather | solution.py:66
  167.5 125.9 %reduce-scatter.2.cloned.1.call-start = ((), (), s32[]{:S(2)}) async-start(), calls=%async_computation.3 | async-start | bytes 786432 | tf_op jit(solution)/shard_map/reduce_scatter | solution.py:73
  254.1 16.9 %copy-start.1 = (f32[2,1]{0,1:T(1,128)S(1)}, f32[2,1]{0,1:T(1,128)}, u32[]{:S(2)}) copy-start(f32[2,1]{0,1:T(1,128)} %param.7) | copy-start | bytes 28
Sparse Core Ops, SparseCore 0:
  27.2 140.2 all-gather.3
  169.6 30.8 all-gather.5
  271.0 22.3 reduce-scatter.1
